TPU v7x, 512 devices: a whole 4x8x8 slice. The times are simulated.
512 devices in a mesh: gx: 32 (over x, y), gy: 16 (over z, core).
Axes of the slice: x: 4, y: 8, z: 8, core: 2. Of those that a mesh axis runs over, the one named last changes fastest.
Arguments:
- right_side: bfloat16 [32, 16, 896, 128], P('gx', 'gy')
- schur_offdiag: bfloat16 [32, 16, 896, 896], P('gx', 'gy'), may hold values from -0.125 to 0.125
- schur_diag: float32 [32, 16, 896], P('gx', 'gy'), may hold values from 1.5 to 3
- trace_offdiag: bfloat16 [32, 16, 896, 896], P('gx', 'gy'), may hold values from -0.0390625 to 0.0390625
- trace_diag: float32 [32, 16, 896], P('gx', 'gy'), may hold values from 0.3 to 0.7
- couplings: bfloat16 [32, 16, 4, 128, 128], P('gx', 'gy'), may hold values from -0.375 to 0.375
- margin_rows: int32 [32, 16, 4, 128], P('gx', 'gy'), may hold values from 0 to 895, as said below
- deflation: bfloat16 [32, 16, 8, 896], P('gx', 'gy'), may hold values from -0.59765625 to 0.59765625
- coarse_inverse: float32 [4096, 4096], P(('gx', 'gy'))
- coarse_map: int32 [4096], replicated, may hold values from 0 to 4095, each once
Outputs:
- solution: float32 [32, 16, 896, 128], P('gx', 'gy')
- residual: float32 [32, 16, 896, 128], P('gx', 'gy')
Inputs may be any that keep to these rules, and one draw needn't show every extreme that they name: `margin_rows`: the 512 rows of one subdomain's four lists are all distinct. `coarse_map`: every coarse number appears once.
All inputs are finite; a program needn't handle non-finite values.
Results may differ from a plain program's by a relative error of at most 0.022.
Values may be sent and summed in bfloat16 or wider, within the bound.
No kernel may reach another device: no remote copies, remote signals or barrier semaphores. Data moves between devices by JAX's collectives and lax.ppermute only.
A program may use at most 64 MiB of HBM per device.

v0:
```python
import jax
import jax.numpy as jnp
from jax import lax
from jax.sharding import PartitionSpec as P

ITERS = 3


def from_behind(value, axis, steps):
    count = lax.axis_size(axis)
    leading, last = (max(0, -steps), min(count, count - steps))
    return lax.ppermute(value, axis, [(source, source + steps) for source in range(leading, last)])


def pass_columns(rows, offset):
    return from_behind(rows, "gx", offset)


def pass_lines(rows, offset):
    return from_behind(rows, "gy", offset)


def shards(
    right_side,
    schur_offdiag,
    schur_diag,
    trace_offdiag,
    trace_diag,
    couplings,
    margin_rows,
    deflation,
    coarse_inverse,
    coarse_map,
):
    rhs_wide = right_side[0, 0].astype(jnp.float32)
    schur_mat = schur_offdiag[0, 0]
    schur_scale = schur_diag[0, 0][:, None]
    trace_mat = trace_offdiag[0, 0]
    trace_scale = trace_diag[0, 0][:, None]
    coupling_blocks = couplings[0, 0]
    rows_lists = margin_rows[0, 0]
    flat_rows = rows_lists.reshape(-1)
    vectors = deflation[0, 0]
    vectors_wide = vectors.astype(jnp.float32).T
    coarse_cols = jnp.take(coarse_inverse, coarse_map, axis=1)

    def apply_schur(field):
        rounded = lax.optimization_barrier(field.astype(jnp.bfloat16))
        result = schur_scale * rounded.astype(jnp.float32) + jnp.dot(
            schur_mat, rounded, preferred_element_type=jnp.float32
        )
        sent_rows = rounded[rows_lists]
        received = jnp.stack(
            [
                pass_columns(sent_rows[1], 1),
                pass_columns(sent_rows[0], -1),
                pass_lines(sent_rows[3], 1),
                pass_lines(sent_rows[2], -1),
            ]
        )
        coupled = jnp.einsum(
            "dab,dbs->das", coupling_blocks, received, preferred_element_type=jnp.float32
        )
        return result.at[flat_rows].add(-coupled.reshape(-1, coupled.shape[-1]))

    def apply_prec(field):
        rounded = lax.optimization_barrier(field.astype(jnp.bfloat16))
        result = trace_scale * rounded.astype(jnp.float32) + jnp.dot(
            trace_mat, rounded, preferred_element_type=jnp.float32
        )
        coarse = jnp.dot(vectors, rounded, preferred_element_type=jnp.float32)
        stacked = lax.all_gather(coarse, ("gx", "gy"), axis=0, tiled=True)
        solved = jnp.dot(coarse_cols, stacked, precision=lax.Precision.HIGHEST)
        return result + jnp.dot(vectors_wide, solved, precision=lax.Precision.HIGHEST)

    solution = jnp.zeros(rhs_wide.shape, jnp.float32)
    direction = apply_prec(rhs_wide)
    for iteration in range(ITERS):
        image = apply_schur(direction)
        mapped = apply_prec(image)
        numer, denom = lax.psum(
            (jnp.sum(mapped * direction, axis=0), jnp.sum(mapped * mapped, axis=0)), ("gx", "gy")
        )
        alpha = numer / denom
        solution = solution + alpha * direction
        direction = direction - alpha * mapped
    residual = rhs_wide - apply_schur(solution)
    return (solution[None, None], residual[None, None])


def solution(mesh):
    return jax.shard_map(
        shards,
        mesh=mesh,
        in_specs=(
            P("gx", "gy", None, None),
            P("gx", "gy", None, None),
            P("gx", "gy", None),
            P("gx", "gy", None, None),
            P("gx", "gy", None),
            P("gx", "gy", None, None, None),
            P("gx", "gy", None, None),
            P("gx", "gy", None, None),
            P(("gx", "gy"), None),
            P(),
        ),
        out_specs=(P("gx", "gy", None, None), P("gx", "gy", None, None)),
        check_vma=False,
    )
```

profile of v0, /device:TPU:3, one launch (start us, length us, event | category | flops | bytes accessed | tf_op | source)
XLA Modules:
  0.0 902.4 jit_solution(9823042556222363306)
XLA Ops:
  9.1 2.8 copy.24
  12.1 15.7 %gather_fusion = f32[4096,8]{1,0:T(8,128)} fusion(f32[8,4096]{0,1:T(8,128)} %copy.24, s32[4096]{0:T(1024)S(1)} %fusion.131), kind=kCustom, calls=%fused_computation | custom fusion | bytes 278528 | tf_op jit(solution)/shard_map/jit(_take)/gather | solution.py:45
  27.8 105.3 %all-gather.5.cloned.1.call-done = f32[4096,128]{1,0:T(8,128)} async-done(((f32[8,128]{1,0:T(8,128)}), f32[4096,128]{1,0:T(8,128)}) %all-gather.5.cloned.1.call-update) | async-done | bytes 2097168 | tf_op jit(solution)/shard_map/all_gather | solution.py:72
  133.1 6.4 fusion.4
  144.1 3.1 collective-permute-start
  147.2 4.3 collective-permute-start.1
  151.5 3.4 collective-permute-start.2
  158.2 1.9 collective-permute-done.3
  161.0 5.2 scatter_fusion
  168.2 111.2 %all-gather.7.cloned.1.call-done = f32[4096,128]{1,0:T(8,128)} async-done(((f32[8,128]{1,0:T(8,128)}), f32[4096,128]{1,0:T(8,128)}) %all-gather.7.cloned.1.call-update) | async-done | bytes 2097168 | tf_op jit(solution)/shard_map/all_gather | solution.py:72
  279.4 6.4 fusion.2
  287.7 95.9 %all-reduce.2 = (f32[128]{0:T(128)S(1)}, f32[128]{0:T(128)S(1)}) all-reduce(f32[128]{0:T(128)S(1)} %get-tuple-element.7, f32[128]{0:T(128)S(1)} %get-tuple-element.6), channel_id=1, replica_groups=mesh['gx'=32,'gy'=16] {'gx','gy'}, use_global_device_ids=true, to_apply=%region_2.3 | all-reduce | flops 256 | bytes 2048 | tf_op jit(solution)/shard_map/psum | solution.py:81
  383.5 2.0 fusion.142
  390.2 5.5 collective-permute-start.5
  395.7 3.0 collective-permute-start.6
  402.0 1.9 collective-permute-done.7
  404.8 5.2 scatter_fusion.1
  412.1 110.5 %all-gather.9.cloned.1.call-done = f32[4096,128]{1,0:T(8,128)} async-done(((f32[8,128]{1,0:T(8,128)}), f32[4096,128]{1,0:T(8,128)}) %all-gather.9.cloned.1.call-update) | async-done | bytes 2097168 | tf_op jit(solution)/shard_map/all_gather | solution.py:72
  522.5 6.4 fusion
  530.8 95.9 %all-reduce.1 = (f32[128]{0:T(128)S(1)}, f32[128]{0:T(128)S(1)}) all-reduce(f32[128]{0:T(128)S(1)} %get-tuple-element.5, f32[128]{0:T(128)S(1)} %get-tuple-element.4), channel_id=1, replica_groups=mesh['gx'=32,'gy'=16] {'gx','gy'}, use_global_device_ids=true, to_apply=%region_7.8 | all-reduce | flops 256 | bytes 2048 | tf_op jit(solution)/shard_map/psum | solution.py:81
  632.6 5.5 collective-permute-start.9
  638.1 3.0 collective-permute-start.10
  644.4 1.9 collective-permute-done.11
  647.2 5.2 scatter_fusion.2
  654.2 110.7 %all-gather.11.cloned.1.call-done = f32[4096,128]{1,0:T(8,128)} async-done(((f32[8,128]{1,0:T(8,128)}), f32[4096,128]{1,0:T(8,128)}) %all-gather.11.cloned.1.call-update) | async-done | bytes 2097168 | tf_op jit(solution)/shard_map/all_gather | solution.py:72
  764.9 6.4 fusion.6
  772.5 95.9 %all-reduce = (f32[128]{0:T(128)S(1)}, f32[128]{0:T(128)S(1)}) all-reduce(f32[128]{0:T(128)S(1)} %get-tuple-element.3, f32[128]{0:T(128)S(1)} %get-tuple-element.2), channel_id=1, replica_groups=mesh['gx'=32,'gy'=16] {'gx','gy'}, use_global_device_ids=true, to_apply=%region_12.13 | all-reduce | flops 256 | bytes 2048 | tf_op jit(solution)/shard_map/psum | solution.py:81
  868.4 2.2 fusion.141
  875.3 5.5 collective-permute-start.13
  880.8 3.0 collective-permute-start.14
  887.1 1.9 collective-permute-done.15
  889.2 4.8 scatter_fusion.3
  (104 shorter events, 50.3 us)
Async XLA Ops:
  7.2 132.8 %copy-start = (bf16[1,1,896,896]{3,2,1,0:T(8,128)(2,1)S(1)}, bf16[1,1,896,896]{3,2,1,0:T(8,128)(2,1)}, u32[]{:S(2)}) copy-start(bf16[1,1,896,896]{3,2,1,0:T(8,128)(2,1)} %param.13) | copy-start | bytes 4816900
  7.2 20.6 %copy-start.10 = (s32[1,1,4,128]{3,2,1,0:T(4,128)S(1)}, s32[1,1,4,128]{3,2,1,0:T(4,128)}, u32[]{:S(2)}) copy-start(s32[1,1,4,128]{3,2,1,0:T(4,128)} %param.16) | copy-start | bytes 6148
  7.2 125.9 %all-gather.5.cloned.1.call-start = ((), (), s32[]{:S(2)}) async-start(), calls=%async_computation | async-start | bytes 2101248 | tf_op jit(solution)/shard_map/all_gather | solution.py:72
  9.1 270.3 %all-gather.7.cloned.1.call-start = ((), (), s32[]{:S(2)}) async-start(), calls=%async_computation.1 | async-start | bytes 2101248 | tf_op jit(solution)/shard_map/all_gather | solution.py:72
  27.8 111.7 %copy-start.8 = (bf16[1,1,8,896]{3,2,1,0:T(8,128)(2,1)S(1)}, bf16[1,1,8,896]{3,2,1,0:T(8,128)(2,1)}, u32[]{:S(2)}) copy-start(bf16[1,1,8,896]{3,2,1,0:T(8,128)(2,1)} %param.17) | copy-start | bytes 43012
  140.0 16.9 %copy-start.1 = (bf16[1,1,896,896]{3,2,1,0:T(8,128)(2,1)S(1)}, bf16[1,1,896,896]{3,2,1,0:T(8,128)(2,1)}, u32[]{:S(2)}) copy-start(bf16[1,1,896,896]{3,2,1,0:T(8,128)(2,1)} %param.11) | copy-start | bytes 4816900
  143.3 16.9 %copy-start.13 = (bf16[1,1,4,128,128]{4,3,2,1,0:T(8,128)(2,1)S(1)}, bf16[1,1,4,128,128]{4,3,2,1,0:T(8,128)(2,1)}, u32[]{:S(2)}) copy-start(bf16[1,1,4,128,128]{4,3,2,1,0:T(8,128)(2,1)} %param.15) | copy-start | bytes 393220
  144.1 14.1 %collective-permute-start = (bf16[128,128]{1,0:T(8,128)(2,1)S(1)}, bf16[128,128]{1,0:T(8,128)(2,1)S(1)}, u32[]{:S(2)}, u32[]{:S(2)}) collective-permute-start(bf16[128,128]{1,0:T(8,128)(2,1)S(1)} %get-tuple-element.30), channel_id=1, source_target_pairs={{0,16},{16,32},{32,48},{48,64},{64,80},{80,96},{96,112},{112,128},... | collective-permute-start | bytes 98312 | tf_op jit(solution)/shard_map/ppermute | solution.py:12
  147.2 11.0 %collective-permute-start.1 = (bf16[128,128]{1,0:T(8,128)(2,1)S(1)}, bf16[128,128]{1,0:T(8,128)(2,1)S(1)}, u32[]{:S(2)}, u32[]{:S(2)}) collective-permute-start(bf16[128,128]{1,0:T(8,128)(2,1)S(1)} %get-tuple-element.32), channel_id=1, source_target_pairs={{16,0},{32,16},{48,32},{64,48},{80,64},{96,80},{112,96},{128,112},... | collective-permute-start | bytes 98312 | tf_op jit(solution)/shard_map/ppermute | solution.py:12
  151.5 6.7 collective-permute-start.2
  154.9 5.2 collective-permute-start.3
  168.0 354.6 %all-gather.9.cloned.1.call-start = ((), (), s32[]{:S(2)}) async-start(), calls=%async_computation.2 | async-start | bytes 2101248 | tf_op jit(solution)/shard_map/all_gather | solution.py:72
  279.4 6.9 copy-start.5
  387.4 16.5 %copy-start.14 = (bf16[1,1,4,128,128]{4,3,2,1,0:T(8,128)(2,1)S(1)}, bf16[1,1,4,128,128]{4,3,2,1,0:T(8,128)(2,1)}, u32[]{:S(2)}) copy-start(bf16[1,1,4,128,128]{4,3,2,1,0:T(8,128)(2,1)} %param.15) | copy-start | bytes 393220
  388.3 13.7 %collective-permute-start.4 = (bf16[128,128]{1,0:T(8,128)(2,1)S(1)}, bf16[128,128]{1,0:T(8,128)(2,1)S(1)}, u32[]{:S(2)}, u32[]{:S(2)}) collective-permute-start(bf16[128,128]{1,0:T(8,128)(2,1)S(1)} %get-tuple-element.26), channel_id=1, source_target_pairs={{0,16},{16,32},{32,48},{48,64},{64,80},{80,96},{96,112},{112,128},... | collective-permute-start | bytes 98312 | tf_op jit(solution)/shard_map/ppermute | solution.py:12
  390.2 11.8 %collective-permute-start.5 = (bf16[128,128]{1,0:T(8,128)(2,1)S(1)}, bf16[128,128]{1,0:T(8,128)(2,1)S(1)}, u32[]{:S(2)}, u32[]{:S(2)}) collective-permute-start(bf16[128,128]{1,0:T(8,128)(2,1)S(1)} %get-tuple-element.28), channel_id=1, source_target_pairs={{16,0},{32,16},{48,32},{64,48},{80,64},{96,80},{112,96},{128,112},... | collective-permute-start | bytes 98312 | tf_op jit(solution)/shard_map/ppermute | solution.py:12
  395.7 6.3 collective-permute-start.6
  398.7 5.2 collective-permute-start.7
  411.8 353.1 %all-gather.11.cloned.1.call-start = ((), (), s32[]{:S(2)}) async-start(), calls=%async_computation.3 | async-start | bytes 2101248 | tf_op jit(solution)/shard_map/all_gather | solution.py:72
  522.5 6.9 copy-start.2
  629.8 16.5 %copy-start.15 = (bf16[1,1,4,128,128]{4,3,2,1,0:T(8,128)(2,1)S(1)}, bf16[1,1,4,128,128]{4,3,2,1,0:T(8,128)(2,1)}, u32[]{:S(2)}) copy-start(bf16[1,1,4,128,128]{4,3,2,1,0:T(8,128)(2,1)} %param.15) | copy-start | bytes 393220
  630.7 13.7 %collective-permute-start.8 = (bf16[128,128]{1,0:T(8,128)(2,1)S(1)}, bf16[128,128]{1,0:T(8,128)(2,1)S(1)}, u32[]{:S(2)}, u32[]{:S(2)}) collective-permute-start(bf16[128,128]{1,0:T(8,128)(2,1)S(1)} %get-tuple-element.22), channel_id=1, source_target_pairs={{0,16},{16,32},{32,48},{48,64},{64,80},{80,96},{96,112},{112,128},... | collective-permute-start | bytes 98312 | tf_op jit(solution)/shard_map/ppermute | solution.py:12
  632.6 11.8 %collective-permute-start.9 = (bf16[128,128]{1,0:T(8,128)(2,1)S(1)}, bf16[128,128]{1,0:T(8,128)(2,1)S(1)}, u32[]{:S(2)}, u32[]{:S(2)}) collective-permute-start(bf16[128,128]{1,0:T(8,128)(2,1)S(1)} %get-tuple-element.24), channel_id=1, source_target_pairs={{16,0},{32,16},{48,32},{64,48},{80,64},{96,80},{112,96},{128,112},... | collective-permute-start | bytes 98312 | tf_op jit(solution)/shard_map/ppermute | solution.py:12
  638.1 6.3 collective-permute-start.10
  641.1 5.2 collective-permute-start.11
  764.9 6.9 copy-start.3
  764.9 6.9 copy-start.4
  872.5 16.5 %copy-start.16 = (bf16[1,1,4,128,128]{4,3,2,1,0:T(8,128)(2,1)S(1)}, bf16[1,1,4,128,128]{4,3,2,1,0:T(8,128)(2,1)}, u32[]{:S(2)}) copy-start(bf16[1,1,4,128,128]{4,3,2,1,0:T(8,128)(2,1)} %param.15) | copy-start | bytes 393220
  873.4 13.7 %collective-permute-start.12 = (bf16[128,128]{1,0:T(8,128)(2,1)S(1)}, bf16[128,128]{1,0:T(8,128)(2,1)S(1)}, u32[]{:S(2)}, u32[]{:S(2)}) collective-permute-start(bf16[128,128]{1,0:T(8,128)(2,1)S(1)} %get-tuple-element.18), channel_id=1, source_target_pairs={{0,16},{16,32},{32,48},{48,64},{64,80},{80,96},{96,112},{112,128},... | collective-permute-start | bytes 98312 | tf_op jit(solution)/shard_map/ppermute | solution.py:12
  875.3 11.8 %collective-permute-start.13 = (bf16[128,128]{1,0:T(8,128)(2,1)S(1)}, bf16[128,128]{1,0:T(8,128)(2,1)S(1)}, u32[]{:S(2)}, u32[]{:S(2)}) collective-permute-start(bf16[128,128]{1,0:T(8,128)(2,1)S(1)} %get-tuple-element.20), channel_id=1, source_target_pairs={{16,0},{32,16},{48,32},{64,48},{80,64},{96,80},{112,96},{128,112},... | collective-permute-start | bytes 98312 | tf_op jit(solution)/shard_map/ppermute | solution.py:12
  880.8 6.3 collective-permute-start.14
  883.8 5.2 collective-permute-start.15
  (5 other events, 26.2 us)
Sparse Core Ops, SparseCore 0:
  12.8 120.2 all-gather.4
  168.1 111.2 all-gather.6
  411.9 110.5 all-gather.8
  654.3 110.5 all-gather.10
where the time goes:
time: 904 us; the launch traced here: 902 us
  waiting for transfers between devices  445 us (49%)
  blocking collectives  288 us (32%)
  starting transfers between devices  50.2 us (6%)
  matrix products  44.5 us (5%)
  other arithmetic  30.7 us (3%)
  local copies, waits for them, and re-layouts  29.7 us (3%)
  between operations  14.2 us (2%)
    all_gather x4, waiting for transfers between devices, apply_prec(): stacked = lax.all_gather(coarse, ('gx', 'gy'), axis=0, tiled=True)  438 us
    psum x3, blocking collectives, shards(): lax.psum((jnp.sum(mapped * direction, axis=0), jnp.sum(mapped * mapped, a...  288 us
    ppermute x16, starting transfers between devices, from_behind(): lax.ppermute(value, axis, [(source, source + steps) for source in range(l...  49.6 us
    dot_general x4, matrix products, apply_prec(): solved = jnp.dot(coarse_cols, stacked, precision=lax.Precision.HIGHEST)  25.7 us
    scatter-add x4, other arithmetic, apply_schur(): return result.at[flat_rows].add(-coupled.reshape(-1, coupled.shape[-1]))  20.3 us
  transfers between devices with their start and end apart: 20, of which 8 were waited for; matrix products, arithmetic and copies ran while one was open for 3% of the time, Pallas kernels for 0%

commit v1 on v0

--- a/solution.py
+++ b/solution.py
@@ -69,7 +69,10 @@
             trace_mat, rounded, preferred_element_type=jnp.float32
         )
         coarse = jnp.dot(vectors, rounded, preferred_element_type=jnp.float32)
-        stacked = lax.all_gather(coarse, ("gx", "gy"), axis=0, tiled=True)
+        stacked = jnp.concatenate(
+            lax.all_to_all(jnp.stack([coarse] * lax.axis_size(("gx", "gy"))), ("gx", "gy"), 0, 0),
+            axis=0,
+        )
         solved = jnp.dot(coarse_cols, stacked, precision=lax.Precision.HIGHEST)
         return result + jnp.dot(vectors_wide, solved, precision=lax.Precision.HIGHEST)
 

time: 904 us -> 702 us (0.78)
  waiting for transfers between devices: 445 us -> 40.6 us
  blocking collectives: 288 us -> 478 us
  starting transfers between devices: 50.2 us -> 75.7 us
  between operations: 14.2 us -> 1.31 us
    all_gather x4 -> x0, waiting for transfers between devices: 438 us -> none  [apply_prec(): stacked = lax.all_gather(coarse, ('gx', 'gy'), axis=0, tiled=True)]
    all_to_all x0 -> x3, blocking collectives: none -> 189 us  [apply_prec(): lax.all_to_all(jnp.stack([coarse] * lax.axis_size(('gx', 'gy'))), ('gx',...]
    all_to_all x0 -> x1, waiting for transfers between devices: none -> 32.9 us  [apply_prec(): lax.all_to_all(jnp.stack([coarse] * lax.axis_size(('gx', 'gy'))), ('gx',...]
    all_to_all x0 -> x1, starting transfers between devices: none -> 23.6 us  [apply_prec(): lax.all_to_all(jnp.stack([coarse] * lax.axis_size(('gx', 'gy'))), ('gx',...]
  transfers between devices with their start and end apart: 20 -> 17, of which waited for: 8 -> 5; matrix products, arithmetic and copies ran while one was open for 3% -> 3% of each run, Pallas kernels for 0% -> 0%
where the time goes in v1:
time: 702 us; the launch traced here: 692 us
  blocking collectives  478 us (68%)
  starting transfers between devices  75.7 us (11%)
  waiting for transfers between devices  40.6 us (6%)
  matrix products  35.7 us (5%)
  local copies, waits for them, and re-layouts  30.7 us (4%)
  other arithmetic  30.7 us (4%)
    psum x3, blocking collectives, shards(): lax.psum((jnp.sum(mapped * direction, axis=0), jnp.sum(mapped * mapped, a...  288 us
    all_to_all x3, blocking collectives, apply_prec(): lax.all_to_all(jnp.stack([coarse] * lax.axis_size(('gx', 'gy'))), ('gx',...  189 us
    ppermute x16, starting transfers between devices, from_behind(): lax.ppermute(value, axis, [(source, source + steps) for source in range(l...  52.1 us
    all_to_all x1, waiting for transfers between devices, apply_prec(): lax.all_to_all(jnp.stack([coarse] * lax.axis_size(('gx', 'gy'))), ('gx',...  32.9 us
    all_to_all x1, starting transfers between devices, apply_prec(): lax.all_to_all(jnp.stack([coarse] * lax.axis_size(('gx', 'gy'))), ('gx',...  23.6 us
    scatter-add x4, other arithmetic, apply_schur(): return result.at[flat_rows].add(-coupled.reshape(-1, coupled.shape[-1]))  20.3 us
    dot_general x4, matrix products, apply_prec(): solved = jnp.dot(coarse_cols, stacked, precision=lax.Precision.HIGHEST)  19.2 us
    gather x1, local copies, waits for them, and re-layouts, shards(): coarse_cols = jnp.take(coarse_inverse, coarse_map, axis=1)  15.7 us
  transfers between devices with their start and end apart: 17, of which 5 were waited for; matrix products, arithmetic and copies ran while one was open for 3% of the time, Pallas kernels for 0%

profile of v1, /device:TPU:3, one launch (start us, length us, event | category | flops | bytes accessed | tf_op | source)
XLA Modules:
  0.0 692.4 jit_solution(16561879557193525579)
XLA Ops:
  3.3 23.6 %all-to-all-start = ((f32[512,8,128]{2,1,0:T(8,128)}), f32[512,8,128]{2,1,0:T(8,128)}, u32[]{:S(2)}, u32[]{:S(2)}) async-start(f32[512,8,128]{2,1,0:T(8,128)} %stack.48), calls=%async_computation | async-start | bytes 4194304 | tf_op jit(solution)/shard_map/all_to_all | solution.py:73
  27.0 2.0 copy.12
  29.0 15.7 %gather_fusion = f32[4096,8]{1,0:T(8,128)} fusion(f32[8,4096]{0,1:T(8,128)} %copy.12, s32[4096]{0:T(1024)S(1)} %fusion.135), kind=kCustom, calls=%fused_computation | custom fusion | bytes 278528 | tf_op jit(solution)/shard_map/jit(_take)/gather | solution.py:45
  44.7 32.9 %all-to-all-done = f32[512,8,128]{2,1,0:T(8,128)} async-done(((f32[512,8,128]{2,1,0:T(8,128)}), f32[512,8,128]{2,1,0:T(8,128)}, u32[]{:S(2)}, u32[]{:S(2)}) %all-to-all-start) | async-done | bytes 2097184 | tf_op jit(solution)/shard_map/all_to_all | solution.py:73
  77.6 6.4 fusion.6
  88.6 3.8 collective-permute-start
  92.4 2.7 collective-permute-start.2
  95.1 5.1 collective-permute-start.1
  106.4 5.2 scatter_fusion
  112.9 62.0 %all_to_all.20 = f32[512,8,128]{2,1,0:T(8,128)S(1)} all-to-all(f32[512,8,128]{2,1,0:T(8,128)S(1)} %stack.54), channel_id=1, replica_groups=mesh['gx'=32,'gy'=16] {'gx','gy'}, dimensions={0} | all-to-all | bytes 4194304 | tf_op jit(solution)/shard_map/all_to_all | solution.py:73
  174.9 4.3 fusion.4
  181.0 96.1 %all-reduce.2 = (f32[128]{0:T(128)S(1)}, f32[128]{0:T(128)S(1)}) all-reduce(f32[128]{0:T(128)S(1)} %get-tuple-element.7, f32[128]{0:T(128)S(1)} %get-tuple-element.6), channel_id=1, replica_groups=mesh['gx'=32,'gy'=16] {'gx','gy'}, use_global_device_ids=true, to_apply=%region_2.3 | all-reduce | flops 256 | bytes 2048 | tf_op jit(solution)/shard_map/psum | solution.py:84
  277.1 2.0 fusion.146
  281.8 2.6 collective-permute-start.4
  284.4 2.9 collective-permute-start.6
  287.3 5.4 collective-permute-start.5
  298.9 5.2 scatter_fusion.1
  305.4 63.7 %all_to_all.21 = f32[512,8,128]{2,1,0:T(8,128)S(1)} all-to-all(f32[512,8,128]{2,1,0:T(8,128)S(1)} %stack.60), channel_id=1, replica_groups=mesh['gx'=32,'gy'=16] {'gx','gy'}, dimensions={0} | all-to-all | bytes 4194304 | tf_op jit(solution)/shard_map/all_to_all | solution.py:73
  369.1 4.3 fusion.2
  375.2 96.1 %all-reduce.1 = (f32[128]{0:T(128)S(1)}, f32[128]{0:T(128)S(1)}) all-reduce(f32[128]{0:T(128)S(1)} %get-tuple-element.5, f32[128]{0:T(128)S(1)} %get-tuple-element.4), channel_id=1, replica_groups=mesh['gx'=32,'gy'=16] {'gx','gy'}, use_global_device_ids=true, to_apply=%region_7.8 | all-reduce | flops 256 | bytes 2048 | tf_op jit(solution)/shard_map/psum | solution.py:84
  475.3 2.6 collective-permute-start.8
  477.9 2.9 collective-permute-start.10
  480.8 5.4 collective-permute-start.9
  492.4 5.2 scatter_fusion.2
  498.9 63.7 %all_to_all.22 = f32[512,8,128]{2,1,0:T(8,128)S(1)} all-to-all(f32[512,8,128]{2,1,0:T(8,128)S(1)} %stack.66), channel_id=1, replica_groups=mesh['gx'=32,'gy'=16] {'gx','gy'}, dimensions={0} | all-to-all | bytes 4194304 | tf_op jit(solution)/shard_map/all_to_all | solution.py:73
  562.6 4.3 fusion
  568.0 96.1 %all-reduce = (f32[128]{0:T(128)S(1)}, f32[128]{0:T(128)S(1)}) all-reduce(f32[128]{0:T(128)S(1)} %get-tuple-element.3, f32[128]{0:T(128)S(1)} %get-tuple-element.2), channel_id=1, replica_groups=mesh['gx'=32,'gy'=16] {'gx','gy'}, use_global_device_ids=true, to_apply=%region_12.13 | all-reduce | flops 256 | bytes 2048 | tf_op jit(solution)/shard_map/psum | solution.py:84
  664.1 2.2 fusion.145
  669.1 2.6 collective-permute-start.12
  671.7 2.9 collective-permute-start.14
  674.6 5.4 collective-permute-start.13
  685.5 4.8 scatter_fusion.3
  (109 shorter events, 51.2 us)
Async XLA Ops:
  0.6 83.9 %copy-start = (bf16[1,1,896,896]{3,2,1,0:T(8,128)(2,1)S(1)}, bf16[1,1,896,896]{3,2,1,0:T(8,128)(2,1)}, u32[]{:S(2)}) copy-start(bf16[1,1,896,896]{3,2,1,0:T(8,128)(2,1)} %param.13) | copy-start | bytes 4816900
  3.3 23.6 %copy-start.15 = (f32[1,1,896]{2,1,0:T(1,128)S(1)}, f32[1,1,896]{2,1,0:T(1,128)}, u32[]{:S(2)}) copy-start(f32[1,1,896]{2,1,0:T(1,128)} %param.12) | copy-start | bytes 10756
  3.3 23.7 %copy-start.16 = (f32[1,1,896]{2,1,0:T(1,128)S(1)}, f32[1,1,896]{2,1,0:T(1,128)}, u32[]{:S(2)}) copy-start(f32[1,1,896]{2,1,0:T(1,128)} %param.14) | copy-start | bytes 10756
  3.3 23.7 %copy-start.12 = (f32[8,4096]{1,0:T(8,128)S(1)}, f32[8,4096]{1,0:T(8,128)}, u32[]{:S(2)}) copy-start(f32[8,4096]{1,0:T(8,128)} %param.18) | copy-start | bytes 393220
  3.3 74.3 %all-to-all-start = ((f32[512,8,128]{2,1,0:T(8,128)}), f32[512,8,128]{2,1,0:T(8,128)}, u32[]{:S(2)}, u32[]{:S(2)}) async-start(f32[512,8,128]{2,1,0:T(8,128)} %stack.48), calls=%async_computation | async-start | bytes 4194304 | tf_op jit(solution)/shard_map/all_to_all | solution.py:73
  27.0 17.7 %copy-start.14 = (s32[1,1,4,128]{3,2,1,0:T(4,128)S(1)}, s32[1,1,4,128]{3,2,1,0:T(4,128)}, u32[]{:S(2)}) copy-start(s32[1,1,4,128]{3,2,1,0:T(4,128)} %param.16) | copy-start | bytes 6148
  44.7 39.3 %copy-start.11 = (bf16[1,1,8,896]{3,2,1,0:T(8,128)(2,1)S(1)}, bf16[1,1,8,896]{3,2,1,0:T(8,128)(2,1)}, u32[]{:S(2)}) copy-start(bf16[1,1,8,896]{3,2,1,0:T(8,128)(2,1)} %param.17) | copy-start | bytes 43012
  77.6 6.9 copy-start.9
  84.5 17.7 %copy-start.4 = (bf16[1,1,896,896]{3,2,1,0:T(8,128)(2,1)S(1)}, bf16[1,1,896,896]{3,2,1,0:T(8,128)(2,1)}, u32[]{:S(2)}) copy-start(bf16[1,1,896,896]{3,2,1,0:T(8,128)(2,1)} %param.11) | copy-start | bytes 4816900
  87.8 17.7 %copy-start.17 = (bf16[1,1,4,128,128]{4,3,2,1,0:T(8,128)(2,1)S(1)}, bf16[1,1,4,128,128]{4,3,2,1,0:T(8,128)(2,1)}, u32[]{:S(2)}) copy-start(bf16[1,1,4,128,128]{4,3,2,1,0:T(8,128)(2,1)} %param.15) | copy-start | bytes 393220
  88.6 14.9 %collective-permute-start = (bf16[128,128]{1,0:T(8,128)(2,1)S(1)}, bf16[128,128]{1,0:T(8,128)(2,1)S(1)}, u32[]{:S(2)}, u32[]{:S(2)}) collective-permute-start(bf16[128,128]{1,0:T(8,128)(2,1)S(1)} %get-tuple-element.30), channel_id=1, source_target_pairs={{0,16},{16,32},{32,48},{48,64},{64,80},{80,96},{96,112},{112,128},... | collective-permute-start | bytes 98312 | tf_op jit(solution)/shard_map/ppermute | solution.py:12
  92.4 11.2 %collective-permute-start.2 = (bf16[128,128]{1,0:T(8,128)(2,1)S(1)}, bf16[128,128]{1,0:T(8,128)(2,1)S(1)}, u32[]{:S(2)}, u32[]{:S(2)}) collective-permute-start(bf16[128,128]{1,0:T(8,128)(2,1)S(1)} %get-tuple-element.31), channel_id=1, source_target_pairs={{0,1},{1,2},{2,3},{3,4},{4,5},{5,6},{6,7},{7,8},{8,9},{9,10},{10,1... | collective-permute-start | bytes 98312 | tf_op jit(solution)/shard_map/ppermute | solution.py:12
  95.1 8.5 %collective-permute-start.1 = (bf16[128,128]{1,0:T(8,128)(2,1)S(1)}, bf16[128,128]{1,0:T(8,128)(2,1)S(1)}, u32[]{:S(2)}, u32[]{:S(2)}) collective-permute-start(bf16[128,128]{1,0:T(8,128)(2,1)S(1)} %get-tuple-element.32), channel_id=1, source_target_pairs={{16,0},{32,16},{48,32},{64,48},{80,64},{96,80},{112,96},{128,112},... | collective-permute-start | bytes 98312 | tf_op jit(solution)/shard_map/ppermute | solution.py:12
  100.3 5.2 collective-permute-start.3
  112.9 62.0 %copy-start.1 = (f32[4096,8]{1,0:T(8,128)S(1)}, f32[4096,8]{1,0:T(8,128)}, u32[]{:S(2)}) copy-start(f32[4096,8]{1,0:T(8,128)} %gather_fusion) | copy-start | bytes 393220
  280.9 17.1 %copy-start.18 = (bf16[1,1,4,128,128]{4,3,2,1,0:T(8,128)(2,1)S(1)}, bf16[1,1,4,128,128]{4,3,2,1,0:T(8,128)(2,1)}, u32[]{:S(2)}) copy-start(bf16[1,1,4,128,128]{4,3,2,1,0:T(8,128)(2,1)} %param.15) | copy-start | bytes 393220
  281.8 14.3 %collective-permute-start.4 = (bf16[128,128]{1,0:T(8,128)(2,1)S(1)}, bf16[128,128]{1,0:T(8,128)(2,1)S(1)}, u32[]{:S(2)}, u32[]{:S(2)}) collective-permute-start(bf16[128,128]{1,0:T(8,128)(2,1)S(1)} %get-tuple-element.26), channel_id=1, source_target_pairs={{0,16},{16,32},{32,48},{48,64},{64,80},{80,96},{96,112},{112,128},... | collective-permute-start | bytes 98312 | tf_op jit(solution)/shard_map/ppermute | solution.py:12
  284.4 11.6 %collective-permute-start.6 = (bf16[128,128]{1,0:T(8,128)(2,1)S(1)}, bf16[128,128]{1,0:T(8,128)(2,1)S(1)}, u32[]{:S(2)}, u32[]{:S(2)}) collective-permute-start(bf16[128,128]{1,0:T(8,128)(2,1)S(1)} %get-tuple-element.27), channel_id=1, source_target_pairs={{0,1},{1,2},{2,3},{3,4},{4,5},{5,6},{6,7},{7,8},{8,9},{9,10},{10,1... | collective-permute-start | bytes 98312 | tf_op jit(solution)/shard_map/ppermute | solution.py:12
  287.3 8.7 %collective-permute-start.5 = (bf16[128,128]{1,0:T(8,128)(2,1)S(1)}, bf16[128,128]{1,0:T(8,128)(2,1)S(1)}, u32[]{:S(2)}, u32[]{:S(2)}) collective-permute-start(bf16[128,128]{1,0:T(8,128)(2,1)S(1)} %get-tuple-element.28), channel_id=1, source_target_pairs={{16,0},{32,16},{48,32},{64,48},{80,64},{96,80},{112,96},{128,112},... | collective-permute-start | bytes 98312 | tf_op jit(solution)/shard_map/ppermute | solution.py:12
  292.8 5.2 collective-permute-start.7
  305.4 63.7 %copy-start.2 = (f32[4096,8]{1,0:T(8,128)S(1)}, f32[4096,8]{1,0:T(8,128)}, u32[]{:S(2)}) copy-start(f32[4096,8]{1,0:T(8,128)} %gather_fusion) | copy-start | bytes 393220
  474.4 17.1 %copy-start.19 = (bf16[1,1,4,128,128]{4,3,2,1,0:T(8,128)(2,1)S(1)}, bf16[1,1,4,128,128]{4,3,2,1,0:T(8,128)(2,1)}, u32[]{:S(2)}) copy-start(bf16[1,1,4,128,128]{4,3,2,1,0:T(8,128)(2,1)} %param.15) | copy-start | bytes 393220
  475.3 14.3 %collective-permute-start.8 = (bf16[128,128]{1,0:T(8,128)(2,1)S(1)}, bf16[128,128]{1,0:T(8,128)(2,1)S(1)}, u32[]{:S(2)}, u32[]{:S(2)}) collective-permute-start(bf16[128,128]{1,0:T(8,128)(2,1)S(1)} %get-tuple-element.22), channel_id=1, source_target_pairs={{0,16},{16,32},{32,48},{48,64},{64,80},{80,96},{96,112},{112,128},... | collective-permute-start | bytes 98312 | tf_op jit(solution)/shard_map/ppermute | solution.py:12
  477.9 11.6 %collective-permute-start.10 = (bf16[128,128]{1,0:T(8,128)(2,1)S(1)}, bf16[128,128]{1,0:T(8,128)(2,1)S(1)}, u32[]{:S(2)}, u32[]{:S(2)}) collective-permute-start(bf16[128,128]{1,0:T(8,128)(2,1)S(1)} %get-tuple-element.23), channel_id=1, source_target_pairs={{0,1},{1,2},{2,3},{3,4},{4,5},{5,6},{6,7},{7,8},{8,9},{9,10},{10,1... | collective-permute-start | bytes 98312 | tf_op jit(solution)/shard_map/ppermute | solution.py:12
  480.8 8.7 %collective-permute-start.9 = (bf16[128,128]{1,0:T(8,128)(2,1)S(1)}, bf16[128,128]{1,0:T(8,128)(2,1)S(1)}, u32[]{:S(2)}, u32[]{:S(2)}) collective-permute-start(bf16[128,128]{1,0:T(8,128)(2,1)S(1)} %get-tuple-element.24), channel_id=1, source_target_pairs={{16,0},{32,16},{48,32},{64,48},{80,64},{96,80},{112,96},{128,112},... | collective-permute-start | bytes 98312 | tf_op jit(solution)/shard_map/ppermute | solution.py:12
  486.2 5.2 collective-permute-start.11
  498.9 63.7 %copy-start.3 = (f32[4096,8]{1,0:T(8,128)S(1)}, f32[4096,8]{1,0:T(8,128)}, u32[]{:S(2)}) copy-start(f32[4096,8]{1,0:T(8,128)} %gather_fusion) | copy-start | bytes 393220
  668.3 17.1 %copy-start.20 = (bf16[1,1,4,128,128]{4,3,2,1,0:T(8,128)(2,1)S(1)}, bf16[1,1,4,128,128]{4,3,2,1,0:T(8,128)(2,1)}, u32[]{:S(2)}) copy-start(bf16[1,1,4,128,128]{4,3,2,1,0:T(8,128)(2,1)} %param.15) | copy-start | bytes 393220
  669.1 14.3 %collective-permute-start.12 = (bf16[128,128]{1,0:T(8,128)(2,1)S(1)}, bf16[128,128]{1,0:T(8,128)(2,1)S(1)}, u32[]{:S(2)}, u32[]{:S(2)}) collective-permute-start(bf16[128,128]{1,0:T(8,128)(2,1)S(1)} %get-tuple-element.18), channel_id=1, source_target_pairs={{0,16},{16,32},{32,48},{48,64},{64,80},{80,96},{96,112},{112,128},... | collective-permute-start | bytes 98312 | tf_op jit(solution)/shard_map/ppermute | solution.py:12
  671.7 11.6 %collective-permute-start.14 = (bf16[128,128]{1,0:T(8,128)(2,1)S(1)}, bf16[128,128]{1,0:T(8,128)(2,1)S(1)}, u32[]{:S(2)}, u32[]{:S(2)}) collective-permute-start(bf16[128,128]{1,0:T(8,128)(2,1)S(1)} %get-tuple-element.19), channel_id=1, source_target_pairs={{0,1},{1,2},{2,3},{3,4},{4,5},{5,6},{6,7},{7,8},{8,9},{9,10},{10,1... | collective-permute-start | bytes 98312 | tf_op jit(solution)/shard_map/ppermute | solution.py:12
  674.6 8.7 %collective-permute-start.13 = (bf16[128,128]{1,0:T(8,128)(2,1)S(1)}, bf16[128,128]{1,0:T(8,128)(2,1)S(1)}, u32[]{:S(2)}, u32[]{:S(2)}) collective-permute-start(bf16[128,128]{1,0:T(8,128)(2,1)S(1)} %get-tuple-element.20), channel_id=1, source_target_pairs={{16,0},{32,16},{48,32},{64,48},{80,64},{96,80},{112,96},{128,112},... | collective-permute-start | bytes 98312 | tf_op jit(solution)/shard_map/ppermute | solution.py:12
  680.1 5.2 collective-permute-start.15
  (6 other events, 25.7 us)
